TPU v7x, 512 devices: a whole 4x4x16 slice. The times are simulated.
512 devices in a mesh: rep: 32 (over z, core), row: 4 (over x), col: 4 (over y).
Axes of the slice: x: 4, y: 4, z: 16, core: 2. Of those that a mesh axis runs over, the one named last changes fastest.
Arguments:
- coordinates: bfloat16 [128, 32, 3, 128], P('rep')
- resample: int32 [32, 22], P('rep'), may hold values from 0 to 127, as said below
- block_slot: int32 [128], replicated, may hold values from 0 to 127, as said below
- lag_time: int32 [32], P('rep'), may hold values from 1 to 8
- atom_pairs: int32 [2, 4096], replicated, may hold values from 0 to 127, as said below
Outputs:
- instant_cov: bfloat16 [32, 4096, 4096], P('rep', 'row', 'col')
- lagged_cov: bfloat16 [32, 4096, 4096], P('rep', 'row', 'col')
Inputs may be any that keep to these rules, and one draw needn't show every extreme that they name: `resample`: the owner of a block is block_slot // 4. In each replicate at most 2 draws have one owner, and some owner has exactly 2; a block may be drawn more than once. `block_slot`: each slot holds exactly one block. `atom_pairs`: the two atoms of a feature differ, and no unordered pair of atoms appears twice.
All inputs are finite; a program needn't handle non-finite values.
Results may differ from a plain program's by a relative error of at most 0.0073.
Values may be sent and summed in bfloat16 or wider, within the bound.
No kernel may reach another device: no remote copies, remote signals or barrier semaphores. Data moves between devices by JAX's collectives and lax.ppermute only.
A program may use at most 64 MiB of HBM per device.

v0:
```python
import jax
import jax.numpy as jnp
from jax import lax
from jax.sharding import PartitionSpec as P

F = 4096
ATOMS = 128
BLOCK_LEN = 32
DRAWS = 22


def slot_lookup(lists, slot_table):
    matches = lists[..., None] == jnp.arange(slot_table.shape[0], dtype=jnp.int32)
    return jnp.sum(jnp.where(matches, slot_table, 0), axis=-1)


def owner_rank(lists, slot_table, blk_count):
    slots = slot_lookup(lists, slot_table)
    owner_ids = slots // blk_count
    local_ids = slots % blk_count
    draw_ids = jnp.arange(lists.shape[-1], dtype=jnp.int32)
    before = (owner_ids[..., :, None] == owner_ids[..., None, :]) & (
        draw_ids[None, :] < draw_ids[:, None]
    )
    ranks = jnp.sum(before.astype(jnp.int32), axis=-1)
    return (owner_ids, local_ids, ranks)


def pack_requests(resample, block_slot, local_data, capacity):
    every_list = lax.all_gather(resample, "rep", axis=0, tiled=True)
    blk_count = local_data.shape[0]
    owners_all, local_all, ranks_all = owner_rank(every_list, block_slot, blk_count)
    myself = lax.axis_index("rep")
    wanted = (owners_all == myself)[:, :, None] & (
        ranks_all[:, :, None] == jnp.arange(capacity, dtype=jnp.int32)
    )
    picked = local_all[:, :, None] == jnp.arange(blk_count, dtype=jnp.int32)
    selector = jnp.einsum(
        "rdc,rdk->rck", wanted.astype(jnp.float32), picked.astype(jnp.float32)
    ).astype(jnp.bfloat16)
    return jnp.einsum(
        "rck,kx->rcx", selector, local_data, preferred_element_type=jnp.float32
    ).astype(jnp.bfloat16)


def unpack_blocks(received, resample, block_slot, blk_count, capacity):
    owner_ids, local_ids, ranks = owner_rank(resample[0], block_slot, blk_count)
    rows_wanted = owner_ids * capacity + ranks
    flat = received.reshape(-1, received.shape[-1])
    return jnp.take(flat, rows_wanted, axis=0)


def tile_features(chosen, atom_pairs, first_feature, width, shift):
    first_atoms = lax.dynamic_slice_in_dim(atom_pairs[0], first_feature, width)
    second_atoms = lax.dynamic_slice_in_dim(atom_pairs[1], first_feature, width)
    atom_ids = jnp.arange(chosen.shape[-1], dtype=jnp.int32)[:, None]
    signed = (
        (atom_ids == first_atoms[None, :]).astype(jnp.float32)
        - (atom_ids == second_atoms[None, :]).astype(jnp.float32)
    ).astype(jnp.bfloat16)
    flat = chosen.reshape(-1, chosen.shape[-1])
    difference = jnp.dot(flat, signed, preferred_element_type=jnp.float32).reshape(
        DRAWS, BLOCK_LEN, 3, width
    )
    squared = (
        difference[:, :, 0] * difference[:, :, 0]
        + difference[:, :, 1] * difference[:, :, 1]
        + difference[:, :, 2] * difference[:, :, 2]
    )
    features = jnp.sqrt(squared).astype(jnp.bfloat16)
    doubled = jnp.concatenate([features, features], axis=1)
    shifted = lax.dynamic_slice_in_dim(doubled, shift, BLOCK_LEN, axis=1)
    valid_rows = (jnp.arange(BLOCK_LEN, dtype=jnp.int32) < BLOCK_LEN - shift)[None, :, None]
    pair_count = (2 * DRAWS * (BLOCK_LEN - shift)).astype(jnp.float32)
    earlier = jnp.where(valid_rows, features.astype(jnp.float32), 0.0)
    later = jnp.where(valid_rows, shifted.astype(jnp.float32), 0.0)
    feature_mean = (jnp.sum(earlier, axis=(0, 1)) + jnp.sum(later, axis=(0, 1))) / pair_count
    zero_lag = (
        jnp.where(valid_rows, earlier - feature_mean, 0.0).astype(jnp.bfloat16).reshape(-1, width)
    )
    lagged = (
        jnp.where(valid_rows, later - feature_mean, 0.0).astype(jnp.bfloat16).reshape(-1, width)
    )
    return (zero_lag, lagged, pair_count)


def shards(coordinates, resample, block_slot, lag_time, atom_pairs):
    rep_total = lax.axis_size("rep")
    per_owner = (DRAWS + rep_total - 1) // rep_total
    capacity = max(2, per_owner + per_owner // 2)
    blk_count = coordinates.shape[0]
    outgoing = pack_requests(resample, block_slot, coordinates.reshape(blk_count, -1), capacity)
    received = lax.all_to_all(outgoing, "rep", split_axis=0, concat_axis=0, tiled=True)
    chosen = unpack_blocks(received, resample, block_slot, blk_count, capacity).reshape(
        DRAWS, BLOCK_LEN, 3, ATOMS
    )
    width = F // lax.axis_size("row")
    shift = lag_time[0]
    zero_row, lag_row, pair_count = tile_features(
        chosen, atom_pairs, lax.axis_index("row") * width, width, shift
    )
    row_stack = jnp.concatenate([zero_row, lag_row], axis=0)
    zero_col, lag_col, unused_count = tile_features(
        chosen, atom_pairs, lax.axis_index("col") * width, width, shift
    )
    col_stack = jnp.concatenate([zero_col, lag_col], axis=0)
    half_rows = col_stack.shape[0] // 2
    mirrored = jnp.concatenate([col_stack[half_rows:], col_stack[:half_rows]], axis=0)
    instant = (
        jnp.einsum("na,nb->ab", row_stack, col_stack, preferred_element_type=jnp.float32)
        / pair_count
    )
    crossed = (
        jnp.einsum("na,nb->ab", row_stack, mirrored, preferred_element_type=jnp.float32)
        / pair_count
    )
    return (instant[None].astype(jnp.bfloat16), crossed[None].astype(jnp.bfloat16))


def solution(mesh):
    return jax.shard_map(
        shards,
        mesh=mesh,
        in_specs=(P("rep", None, None, None), P("rep", None), P(), P("rep"), P()),
        out_specs=(P("rep", "row", "col"), P("rep", "row", "col")),
        check_vma=False,
    )
```

profile of v0, /device:TPU:1, one launch (start us, length us, event | category | flops | bytes accessed | tf_op | source)
XLA Modules:
  0.0 158.3 jit_solution(3388728040057878747)
XLA Ops:
  0.7 37.5 %all-gather = s32[32,1,22]{2,1,0:T(1,128)S(1)} all-gather(s32[1,1,22]{2,1,0:T(1,128)} %bitcast.64), channel_id=1, replica_groups=mesh['rep'=32,'row'=4,'col'=4] {'rep'}, dimensions={0}, use_global_device_ids=true | all-gather | bytes 2904 | tf_op jit(solution)/shard_map/all_gather | solution.py:30
  38.3 1.2 select_reduce_fusion.2
  40.0 1.0 copy.30
  41.2 0.5 convolution_convert_fusion
  41.8 2.8 %copy.32 = bf16[32,2,12288]{2,1,0:T(2,128)(2,1)} copy(bf16[32,2,12288]{2,0,1:T(8,128)(2,1)S(1)} %convolution_convert_fusion) | data formatting | bytes 3145728 | tf_op jit(solution)/shard_map/convert_element_type | solution.py:43
  44.5 7.0 %all-to-all-start = ((bf16[32,2,12288]{2,1,0:T(2,128)(2,1)}), bf16[32,2,12288]{2,1,0:T(2,128)(2,1)S(1)}, u32[]{:S(2)}, u32[]{:S(2)}) async-start(bf16[32,2,12288]{2,1,0:T(2,128)(2,1)} %copy.32), calls=%async_computation | async-start | bytes 3145728 | tf_op jit(solution)/shard_map/all_to_all | solution.py:93
  52.3 0.2 select_reduce_fusion.3
  52.5 0.2 convert_reduce_fusion.1
  52.8 76.7 %all-to-all-done = bf16[32,2,12288]{2,1,0:T(2,128)(2,1)S(1)} async-done(((bf16[32,2,12288]{2,1,0:T(2,128)(2,1)}), bf16[32,2,12288]{2,1,0:T(2,128)(2,1)S(1)}, u32[]{:S(2)}, u32[]{:S(2)}) %all-to-all-start) | async-done | bytes 1572896 | tf_op jit(solution)/shard_map/all_to_all | solution.py:93
  129.5 0.6 reshape.259
  130.1 0.9 gather_fusion
  131.0 0.8 gather.7
  131.8 0.4 broadcast_select_fusion
  132.2 1.3 fusion.32
  133.5 1.2 fusion.56
  134.8 1.2 fusion.2
  136.0 1.3 fusion.34
  137.3 1.2 fusion.57
  138.5 1.2 fusion.6
  139.7 5.3 %fusion.23 = (f32[1024]{0:T(1024)S(1)}, f32[1024]{0:T(1024)S(1)}, f32[1024]{0:T(1024)S(1)}, f32[1024]{0:T(1024)S(1)}) fusion(pred[32]{0:T(512)(128)(4,1)S(1)} %iota_compare_fusion.9, s32[]{:T(128)S(6)} %select_n.137, bf16[22,32,1024]{2,1,0:T(8,128)(2,1)S(1)} %fusion.57, bf16[22,32,1024]{2,1,0:T(8,128)(2,1)S(1)} %fusion.56, ...), kind=kLoop, calls=%fused_computation.45 | loop fusion | flops 21622784 | bytes 20201508 | tf_op jit(solution)/shard_map/reduce_sum | solution.py:77
  145.0 2.6 %select_convert_fusion.1 = (bf16[22,32,1024]{2,1,0:T(8,128)(2,1)S(1)}, bf16[22,32,1024]{2,1,0:T(8,128)(2,1)S(1)}) fusion(f32[1024]{0:T(1024)S(1)} %get-tuple-element.19, pred[32]{0:T(512)(128)(4,1)S(1)} %iota_compare_fusion.9, s32[]{:T(128)S(6)} %select_n.137, bf16[22,32,1024]{2,1,0:T(8,128)(2,1)S(1)} %fusion.57, f32[1024]{0:T(1024)S(1)} %get-tuple-element.18, ...), kind=kLoop, calls=%fused_computation.43 | loop fusion | flops 11534336 | bytes 5775396 | tf_op jit(solution)/shard_map/convert_element_type | solution.py:82
  147.6 1.4 fusion.21
  149.0 4.7 %fusion.25 = bf16[1,1024,1024]{2,1,0:T(8,128)(2,1)} fusion(f32[]{:T(128)S(6)} %convert_element_type.94, bf16[704,1024]{1,0:T(8,128)(2,1)S(1)} %get-tuple-element.15, bf16[704,1024]{1,0:T(8,128)(2,1)S(1)} %bitcast.57, bf16[704,1024]{1,0:T(8,128)(2,1)S(1)} %bitcast.55, bf16[704,1024]{1,0:T(8,128)(2,1)S(1)} %get-tuple-element.14), kind=kOutput, calls=%fused_computation.48 | convolution fusion | flops 2966421504 | bytes 7864324 | tf_op jit(solution)/shard_map/na,nb->ab/dot_general | solution.py:114
  153.7 4.6 %fusion.24 = bf16[1,1024,1024]{2,1,0:T(8,128)(2,1)} fusion(f32[]{:T(128)S(6)} %convert_element_type.94, bf16[704,1024]{1,0:T(8,128)(2,1)S(1)} %bitcast.58, bf16[704,1024]{1,0:T(8,128)(2,1)S(1)} %get-tuple-element.15, bf16[704,1024]{1,0:T(8,128)(2,1)S(1)} %bitcast.56, bf16[704,1024]{1,0:T(8,128)(2,1)S(1)} %get-tuple-element.14), kind=kOutput, calls=%fused_computation.47 | convolution fusion | flops 2966421504 | bytes 7864324 | tf_op jit(solution)/shard_map/na,nb->ab/dot_general | solution.py:110
  (27 shorter events, 1.0 us)
Async XLA Ops:
  41.7 10.6 %copy-start.1 = (s32[128]{0:T(128)S(1)}, s32[128]{0:T(128)}, u32[]{:S(2)}) copy-start(s32[128]{0:T(128)} %param.7) | copy-start | bytes 1540
  41.8 10.6 %copy-start.2 = (s32[1,22]{1,0:T(1,128)S(1)}, s32[1,22]{1,0:T(1,128)}, u32[]{:S(2)}) copy-start(s32[1,22]{1,0:T(1,128)} %param.6) | copy-start | bytes 268
  41.8 11.0 %copy-start = (s32[2,4096]{1,0:T(2,128)S(1)}, s32[2,4096]{1,0:T(2,128)}, u32[]{:S(2)}) copy-start(s32[2,4096]{1,0:T(2,128)} %param.9) | copy-start | bytes 98308
  44.5 85.0 %all-to-all-start = ((bf16[32,2,12288]{2,1,0:T(2,128)(2,1)}), bf16[32,2,12288]{2,1,0:T(2,128)(2,1)S(1)}, u32[]{:S(2)}, u32[]{:S(2)}) async-start(bf16[32,2,12288]{2,1,0:T(2,128)(2,1)} %copy.32), calls=%async_computation | async-start | bytes 3145728 | tf_op jit(solution)/shard_map/all_to_all | solution.py:93
where the time goes:
time: 159 us; the launch traced here: 158 us
  waiting for transfers between devices  76.7 us (48%)
  blocking collectives  37.5 us (24%)
  other arithmetic  16.4 us (10%)
  matrix products  12.6 us (8%)
  starting transfers between devices  6.98 us (4%)
  local copies, waits for them, and re-layouts  6.61 us (4%)
    all_to_all x1, waiting for transfers between devices, shards(): lax.all_to_all(outgoing, 'rep', split_axis=0, concat_axis=0, tiled=True)  76.7 us
    all_gather x1, blocking collectives, pack_requests(): every_list = lax.all_gather(resample, 'rep', axis=0, tiled=True)  37.5 us
    all_to_all x1, starting transfers between devices, shards(): lax.all_to_all(outgoing, 'rep', split_axis=0, concat_axis=0, tiled=True)  6.98 us
    reduce_sum x1, other arithmetic, tile_features(): jnp.sum(later, axis=(0, 1))  5.29 us
    dot_general x1, matrix products, shards(): jnp.einsum('na,nb->ab', row_stack, mirrored, preferred_element_type=jnp.f...  4.66 us
    dot_general x1, matrix products, shards(): jnp.einsum('na,nb->ab', row_stack, col_stack, preferred_element_type=jnp....  4.65 us
  transfers between devices with their start and end apart: 1, of which 1 were waited for; matrix products, arithmetic and copies ran while one was open for 0% of the time, Pallas kernels for 0%

commit v1 on v0

--- a/solution.py
+++ b/solution.py
@@ -27,7 +27,10 @@
 
 
 def pack_requests(resample, block_slot, local_data, capacity):
-    every_list = lax.all_gather(resample, "rep", axis=0, tiled=True)
+    mid_arr = lax.all_to_all(
+        jnp.stack([resample for _ in range(lax.axis_size("rep"))], axis=0), "rep", 0, 0
+    )
+    every_list = jnp.concatenate(mid_arr, axis=0)
     blk_count = local_data.shape[0]
     owners_all, local_all, ranks_all = owner_rank(every_list, block_slot, blk_count)
     myself = lax.axis_index("rep")

time: 159 us -> 147 us (0.925)
  blocking collectives: 37.5 us -> 0 us
  starting transfers between devices: 6.98 us -> 21.3 us
  waiting for transfers between devices: 76.7 us -> 87.4 us
    all_gather x1 -> x0, blocking collectives: 37.5 us -> none  [pack_requests(): every_list = lax.all_gather(resample, 'rep', axis=0, tiled=True)]
    all_to_all x0 -> x1, starting transfers between devices: none -> 16.7 us  [pack_requests(): lax.all_to_all(jnp.stack([resample for _ in range(lax.axis_size('rep'))],...]
    all_to_all x0 -> x1, waiting for transfers between devices: none -> 10.6 us  [pack_requests(): lax.all_to_all(jnp.stack([resample for _ in range(lax.axis_size('rep'))],...]
    all_to_all x1, starting transfers between devices: 6.98 us -> 4.54 us  [shards(): lax.all_to_all(outgoing, 'rep', split_axis=0, concat_axis=0, tiled=True)]
  transfers between devices with their start and end apart: 1 -> 2, of which waited for: 1 -> 2; matrix products, arithmetic and copies ran while one was open for 0% -> 1% of each run, Pallas kernels for 0% -> 0%
where the time goes in v1:
time: 147 us
  waiting for transfers between devices  87.4 us (59%)
  starting transfers between devices  21.3 us (14%)
  other arithmetic  16.4 us (11%)
  matrix products  12.6 us (9%)
  local copies, waits for them, and re-layouts  7.89 us (5%)
  between operations  1.54 us (1%)
    all_to_all x1, waiting for transfers between devices, shards(): lax.all_to_all(outgoing, 'rep', split_axis=0, concat_axis=0, tiled=True)  76.7 us
    all_to_all x1, starting transfers between devices, pack_requests(): lax.all_to_all(jnp.stack([resample for _ in range(lax.axis_size('rep'))],...  16.7 us
    all_to_all x1, waiting for transfers between devices, pack_requests(): lax.all_to_all(jnp.stack([resample for _ in range(lax.axis_size('rep'))],...  10.6 us
    reduce_sum x1, other arithmetic, tile_features(): jnp.sum(later, axis=(0, 1))  5.29 us
    dot_general x1, matrix products, shards(): jnp.einsum('na,nb->ab', row_stack, mirrored, preferred_element_type=jnp.f...  4.66 us
    dot_general x1, matrix products, shards(): jnp.einsum('na,nb->ab', row_stack, col_stack, preferred_element_type=jnp....  4.65 us
    all_to_all x1, starting transfers between devices, shards(): lax.all_to_all(outgoing, 'rep', split_axis=0, concat_axis=0, tiled=True)  4.54 us
  transfers between devices with their start and end apart: 2, of which 2 were waited for; matrix products, arithmetic and copies ran while one was open for 1% of the time, Pallas kernels for 0%

profile of v1, /device:TPU:1, one launch (start us, length us, event | category | flops | bytes accessed | tf_op | source)
XLA Modules:
  0.0 147.1 jit_solution(7988762982760921713)
XLA Ops:
  0.6 1.3 stack.2
  1.9 16.7 %all-to-all-start = ((s32[32,1,22]{2,1,0:T(1,128)}), s32[32,1,22]{2,1,0:T(1,128)S(1)}, u32[]{:S(2)}, u32[]{:S(2)}) async-start(s32[32,1,22]{2,1,0:T(1,128)} %stack.2), calls=%async_computation | async-start | bytes 32768 | tf_op jit(solution)/shard_map/all_to_all | solution.py:30
  18.7 1.0 copy.41
  19.7 10.6 %all-to-all-done = s32[32,1,22]{2,1,0:T(1,128)S(1)} async-done(((s32[32,1,22]{2,1,0:T(1,128)}), s32[32,1,22]{2,1,0:T(1,128)S(1)}, u32[]{:S(2)}, u32[]{:S(2)}) %all-to-all-start) | async-done | bytes 2848 | tf_op jit(solution)/shard_map/all_to_all | solution.py:30
  30.5 1.2 select_reduce_fusion.2
  32.3 0.5 convolution_convert_fusion
  32.9 2.8 %copy.43 = bf16[32,2,12288]{2,1,0:T(2,128)(2,1)} copy(bf16[32,2,12288]{2,0,1:T(8,128)(2,1)S(1)} %convolution_convert_fusion) | data formatting | bytes 3145728 | tf_op jit(solution)/shard_map/convert_element_type | solution.py:46
  35.7 4.5 %all-to-all-start.1 = ((bf16[32,2,12288]{2,1,0:T(2,128)(2,1)}), bf16[32,2,12288]{2,1,0:T(2,128)(2,1)S(1)}, u32[]{:S(2)}, u32[]{:S(2)}) async-start(bf16[32,2,12288]{2,1,0:T(2,128)(2,1)} %copy.43), calls=%async_computation.1 | async-start | bytes 3145728 | tf_op jit(solution)/shard_map/all_to_all | solution.py:96
  41.5 76.7 %all-to-all-done.1 = bf16[32,2,12288]{2,1,0:T(2,128)(2,1)S(1)} async-done(((bf16[32,2,12288]{2,1,0:T(2,128)(2,1)}), bf16[32,2,12288]{2,1,0:T(2,128)(2,1)S(1)}, u32[]{:S(2)}, u32[]{:S(2)}) %all-to-all-start.1) | async-done | bytes 1572896 | tf_op jit(solution)/shard_map/all_to_all | solution.py:96
  118.3 0.6 reshape.262
  118.9 0.9 gather_fusion
  119.8 0.8 gather.7
  120.6 0.4 broadcast_select_fusion
  121.0 1.3 fusion.32
  122.3 1.2 fusion.56
  123.5 1.2 fusion.2
  124.7 1.3 fusion.34
  126.0 1.2 fusion.57
  127.3 1.2 fusion.6
  128.5 5.3 %fusion.23 = (f32[1024]{0:T(1024)S(1)}, f32[1024]{0:T(1024)S(1)}, f32[1024]{0:T(1024)S(1)}, f32[1024]{0:T(1024)S(1)}) fusion(pred[32]{0:T(512)(128)(4,1)S(1)} %iota_compare_fusion.9, s32[]{:T(128)S(6)} %select_n.137, bf16[22,32,1024]{2,1,0:T(8,128)(2,1)S(1)} %fusion.57, bf16[22,32,1024]{2,1,0:T(8,128)(2,1)S(1)} %fusion.56, ...), kind=kLoop, calls=%fused_computation.45 | loop fusion | flops 21622784 | bytes 20201508 | tf_op jit(solution)/shard_map/reduce_sum | solution.py:80
  133.8 2.6 %select_convert_fusion.1 = (bf16[22,32,1024]{2,1,0:T(8,128)(2,1)S(1)}, bf16[22,32,1024]{2,1,0:T(8,128)(2,1)S(1)}) fusion(f32[1024]{0:T(1024)S(1)} %get-tuple-element.19, pred[32]{0:T(512)(128)(4,1)S(1)} %iota_compare_fusion.9, s32[]{:T(128)S(6)} %select_n.137, bf16[22,32,1024]{2,1,0:T(8,128)(2,1)S(1)} %fusion.57, f32[1024]{0:T(1024)S(1)} %get-tuple-element.18, ...), kind=kLoop, calls=%fused_computation.43 | loop fusion | flops 11534336 | bytes 5775396 | tf_op jit(solution)/shard_map/convert_element_type | solution.py:85
  136.4 1.4 fusion.21
  137.8 4.7 %fusion.25 = bf16[1,1024,1024]{2,1,0:T(8,128)(2,1)} fusion(f32[]{:T(128)S(6)} %convert_element_type.94, bf16[704,1024]{1,0:T(8,128)(2,1)S(1)} %get-tuple-element.15, bf16[704,1024]{1,0:T(8,128)(2,1)S(1)} %bitcast.56, bf16[704,1024]{1,0:T(8,128)(2,1)S(1)} %bitcast.54, bf16[704,1024]{1,0:T(8,128)(2,1)S(1)} %get-tuple-element.14), kind=kOutput, calls=%fused_computation.48 | convolution fusion | flops 2966421504 | bytes 7864324 | tf_op jit(solution)/shard_map/na,nb->ab/dot_general | solution.py:117
  142.5 4.6 %fusion.24 = bf16[1,1024,1024]{2,1,0:T(8,128)(2,1)} fusion(f32[]{:T(128)S(6)} %convert_element_type.94, bf16[704,1024]{1,0:T(8,128)(2,1)S(1)} %bitcast.57, bf16[704,1024]{1,0:T(8,128)(2,1)S(1)} %get-tuple-element.15, bf16[704,1024]{1,0:T(8,128)(2,1)S(1)} %bitcast.55, bf16[704,1024]{1,0:T(8,128)(2,1)S(1)} %get-tuple-element.14), kind=kOutput, calls=%fused_computation.47 | convolution fusion | flops 2966421504 | bytes 7864324 | tf_op jit(solution)/shard_map/na,nb->ab/dot_general | solution.py:113
  (29 shorter events, 1.4 us)
Async XLA Ops:
  1.9 28.5 %all-to-all-start = ((s32[32,1,22]{2,1,0:T(1,128)}), s32[32,1,22]{2,1,0:T(1,128)S(1)}, u32[]{:S(2)}, u32[]{:S(2)}) async-start(s32[32,1,22]{2,1,0:T(1,128)} %stack.2), calls=%async_computation | async-start | bytes 32768 | tf_op jit(solution)/shard_map/all_to_all | solution.py:30
  32.9 8.1 %copy-start.1 = (s32[128]{0:T(128)S(1)}, s32[128]{0:T(128)}, u32[]{:S(2)}) copy-start(s32[128]{0:T(128)} %param.7) | copy-start | bytes 1540
  32.9 8.1 %copy-start.2 = (s32[1,22]{1,0:T(1,128)S(1)}, s32[1,22]{1,0:T(1,128)}, u32[]{:S(2)}) copy-start(s32[1,22]{1,0:T(1,128)} %param.6) | copy-start | bytes 268
  32.9 8.5 %copy-start = (s32[2,4096]{1,0:T(2,128)S(1)}, s32[2,4096]{1,0:T(2,128)}, u32[]{:S(2)}) copy-start(s32[2,4096]{1,0:T(2,128)} %param.9) | copy-start | bytes 98308
  35.7 82.6 %all-to-all-start.1 = ((bf16[32,2,12288]{2,1,0:T(2,128)(2,1)}), bf16[32,2,12288]{2,1,0:T(2,128)(2,1)S(1)}, u32[]{:S(2)}, u32[]{:S(2)}) async-start(bf16[32,2,12288]{2,1,0:T(2,128)(2,1)} %copy.43), calls=%async_computation.1 | async-start | bytes 3145728 | tf_op jit(solution)/shard_map/all_to_all | solution.py:96
